TPU v7x, 256 devices: a whole 4x4x8 slice. The times are simulated.
256 devices in a mesh: expert: 32 (over z_lo, x, core), replica: 8 (over z_hi, y).
Axes of the slice: x: 4, y: 4, z: 8 (z_hi: 2, z_lo: 4; z = z_hi * 4 + z_lo), core: 2. Of those that a mesh axis runs over, the one named last changes fastest.
Arguments:
- tokens: bfloat16 [2048, 4096], P(('expert', 'replica')), may hold values from -6 to 6
- expert_ids: int32 [2048, 8], P(('expert', 'replica')), may hold values from 0 to 31, as said below
- gate_weights: float32 [2048, 8], P(('expert', 'replica')), may hold values from 0.1 to 1
- expert_holder: int32 [32], replicated, may hold values from 0 to 31, each once
- swap_pairs: int32 [8, 2], replicated, may hold values from 0 to 31, as said below
- capacity: int32 [32], replicated, may hold values from 2 to 4, as said below
- w_gate: bfloat16 [32, 1536, 4096], P('expert', 'replica'), may hold values from -0.09375 to 0.09375
- w_up: bfloat16 [32, 1536, 4096], P('expert', 'replica'), may hold values from -0.09375 to 0.09375
- w_down: bfloat16 [32, 1536, 4096], P('expert', 'replica'), may hold values from -0.15625 to 0.15625
Outputs:
- moe_output: bfloat16 [2048, 4096], P(('expert', 'replica'))
- moved_gate: bfloat16 [32, 1536, 4096], P('expert', 'replica')
- moved_up: bfloat16 [32, 1536, 4096], P('expert', 'replica')
- moved_down: bfloat16 [32, 1536, 4096], P('expert', 'replica')
- expert_peak: float32 [32], P('expert')
Inputs may be any that keep to these rules, and one draw needn't show every extreme that they name: `expert_ids`: each token names 8 different experts; among one device's 8 tokens no expert is named more than 4 times, and one expert is named exactly 4 times by the tokens of every device. `swap_pairs`: no index appears twice; the two indices of every pair differ by 16. The expert named 4 times by every device has capacity 4. `expert_holder`: each index of the expert axis holds one expert.
All inputs are finite; a program needn't handle non-finite values.
Results may differ from a plain program's by a relative error of at most 0.014.
Values may be sent and summed in bfloat16 or wider, within the bound.
No kernel may reach another device: no remote copies, remote signals or barrier semaphores. Data moves between devices by JAX's collectives and lax.ppermute only.
A program may use at most 128 MiB of HBM per device.

v0:
```python
import jax
import jax.numpy as jnp
from jax import lax
from jax.sharding import PartitionSpec as P

TOPK = 8
CAP = 4


def pair_partner(swap_pairs, device_count):
    devices = jnp.arange(device_count, dtype=jnp.int32)
    first_dev = swap_pairs[:, 0:1]
    second_dev = swap_pairs[:, 1:2]
    offsets = jnp.where(devices[None, :] == first_dev, second_dev - first_dev, 0)
    offsets = offsets + jnp.where(devices[None, :] == second_dev, first_dev - second_dev, 0)
    return devices + jnp.sum(offsets, axis=0)


def table_lookup(values_table, positions):
    matches = positions[..., None] == jnp.arange(values_table.shape[0], dtype=jnp.int32)
    return jnp.sum(jnp.where(matches, values_table, 0), axis=-1)


def route_slots(expert_ids, holder_now, capacity):
    expert_count = holder_now.shape[0]
    flat_ids = expert_ids.reshape(-1)
    chosen = (flat_ids[:, None] == jnp.arange(expert_count, dtype=jnp.int32)[None, :]).astype(
        jnp.int32
    )
    earlier = jnp.cumsum(chosen, axis=0) - chosen
    ranking = jnp.sum(earlier * chosen, axis=1)
    slot_kept = ranking < table_lookup(capacity, flat_ids)
    target = table_lookup(holder_now, flat_ids)
    slot_ids = jnp.where(slot_kept, target * CAP + ranking, -1)
    matched = slot_ids[None, :] == jnp.arange(expert_count * CAP, dtype=jnp.int32)[:, None]
    owners = jnp.arange(flat_ids.shape[0], dtype=jnp.int32) // TOPK
    source = jnp.sum(jnp.where(matched, owners[None, :], 0), axis=1)
    filled = jnp.any(matched, axis=1)
    return (jnp.maximum(slot_ids, 0), slot_kept, source, filled)


def expert_hidden(row_block, gate_local, up_local):
    leading = row_block.shape[:-1]
    row_matrix = row_block.reshape(-1, row_block.shape[-1])
    contract = (((1,), (1,)), ((), ()))
    gate_value = lax.dot_general(
        row_matrix, gate_local, contract, preferred_element_type=jnp.float32
    )
    up_value = lax.dot_general(row_matrix, up_local, contract, preferred_element_type=jnp.float32)
    hidden = (jax.nn.silu(gate_value) * up_value).astype(jnp.bfloat16)
    return hidden.reshape(leading + (gate_local.shape[0],))


def shards(
    tokens, expert_ids, gate_weights, expert_holder, swap_pairs, capacity, w_gate, w_up, w_down
):
    experts = lax.axis_size("expert")
    replicas = lax.axis_size("replica")
    tok_rows, width = tokens.shape
    partner = pair_partner(swap_pairs, experts)
    me = lax.axis_index("expert")
    swapped = lax.dynamic_index_in_dim(partner, me, 0, keepdims=False) != me
    half = experts // 2
    ring = [(d, (d + half) % experts) for d in range(experts)]
    arrived = tuple((lax.ppermute(w, "expert", ring) for w in (w_gate, w_up, w_down)))
    moved_gate, moved_up, moved_down = (
        jnp.where(swapped, got, own) for got, own in zip(arrived, (w_gate, w_up, w_down))
    )
    gate_local, up_local, down_local = (w_gate[0], w_up[0], w_down[0])
    group_tokens, group_ids = (
        lax.all_gather(tokens, "replica", axis=0, tiled=True),
        lax.all_gather(expert_ids, "replica", axis=0, tiled=True),
    )
    group_ids = group_ids.reshape(replicas, tok_rows, TOPK)
    slot_all, kept_all, source_all, filled_all = jax.vmap(route_slots, in_axes=(0, None, None))(
        group_ids, expert_holder, capacity
    )
    starts = jnp.arange(replicas, dtype=jnp.int32)[:, None] * tok_rows
    picked = jnp.take(group_tokens, source_all + starts, axis=0)
    outgoing = jnp.where(filled_all[:, :, None], picked, jnp.zeros((), jnp.bfloat16))
    hidden = expert_hidden(
        lax.all_to_all(
            outgoing.reshape(replicas, experts, CAP, width),
            "expert",
            split_axis=1,
            concat_axis=1,
            tiled=True,
        ),
        gate_local,
        up_local,
    )
    replica_index = lax.axis_index("replica")
    slot_of = lax.dynamic_index_in_dim(slot_all, replica_index, 0, keepdims=False)
    slot_kept = lax.dynamic_index_in_dim(kept_all, replica_index, 0, keepdims=False)
    hidden_rows = hidden.reshape(-1, hidden.shape[-1])
    local_peak = jnp.max(jnp.abs(hidden_rows)).astype(jnp.float32)
    summed = lax.psum_scatter(
        jnp.dot(hidden_rows, down_local, preferred_element_type=jnp.float32).astype(jnp.bfloat16),
        "replica",
        scatter_dimension=0,
        tiled=True,
    )
    results = summed.reshape(experts, CAP, width)
    returned = lax.all_to_all(results, "expert", split_axis=0, concat_axis=0, tiled=True)
    fetched = jnp.take(returned.reshape(experts * CAP, width), slot_of, axis=0).reshape(
        tok_rows, TOPK, width
    )
    scales = jnp.where(slot_kept, gate_weights.reshape(-1), jnp.float32(0.0)).reshape(
        tok_rows, TOPK, 1
    )
    moe_output = jnp.sum(scales * fetched, axis=1).astype(jnp.bfloat16)
    group_peak = lax.pmax(local_peak, "replica")
    expert_peak = jnp.where(swapped, lax.ppermute(group_peak, "expert", ring), group_peak)
    return (moe_output, moved_gate, moved_up, moved_down, expert_peak.reshape(1))


def solution(mesh):
    placed = (
        P(("expert", "replica"), None),
        P(("expert", "replica"), None),
        P(("expert", "replica"), None),
        P(),
        P(),
        P(),
        P("expert", "replica", None),
        P("expert", "replica", None),
        P("expert", "replica", None),
    )
    return jax.shard_map(
        shards,
        mesh=mesh,
        in_specs=placed,
        out_specs=(
            P(("expert", "replica"), None),
            P("expert", "replica", None),
            P("expert", "replica", None),
            P("expert", "replica", None),
            P("expert"),
        ),
        check_vma=False,
    )
```

profile of v0, /device:TPU:4, one launch (start us, length us, event | category | flops | bytes accessed | tf_op | source)
XLA Modules:
  0.0 756.1 jit_solution(8081594906752745250)
XLA Ops:
  7.2 0.0 reduce-scatter.2.cloned.1.call-start
  7.2 46.4 %all_gather.6 = s32[64,8]{1,0:T(8,128)S(1)} all-gather(s32[8,8]{1,0:T(8,128)} %param.10), channel_id=1, replica_groups=mesh['expert'=32,'replica'=8] {'replica'}, dimensions={0}, use_global_device_ids=true | all-gather | bytes 2304 | tf_op jit(solution)/shard_map/all_gather | solution.py:72
  53.6 0.1 eq.30
  53.7 0.1 copy.43
  53.8 1.4 fusion.20
  55.1 3.0 select_reduce_fusion.1
  58.2 0.1 copy.44
  58.2 0.2 fusion.13
  58.4 0.2 select_reduce_fusion
  58.5 0.1 copy.47
  58.6 0.1 fusion.18
  58.7 44.8 %all_gather.7 = bf16[64,4096]{1,0:T(8,128)(2,1)S(1)} all-gather(bf16[8,4096]{1,0:T(8,128)(2,1)} %param.9), channel_id=1, replica_groups=mesh['expert'=32,'replica'=8] {'replica'}, dimensions={0}, use_global_device_ids=true | all-gather | bytes 589824 | tf_op jit(solution)/shard_map/all_gather | solution.py:71
  103.5 7.7 %gather_fusion = bf16[1024,4096]{1,0:T(8,128)(2,1)} fusion(bf16[64,4096]{1,0:T(8,128)(2,1)S(1)} %all_gather.7, s32[1024]{0:T(1024)S(1)} %fusion.18), kind=kCustom, calls=%fused_computation | custom fusion | bytes 16781312 | tf_op jit(solution)/shard_map/jit(_take)/gather | solution.py:79
  111.3 13.1 %gather.13 = bf16[8,32,4,4096]{3,2,1,0:T(4,128)(2,1)} reshape(bf16[1024,4096]{1,0:T(8,128)(2,1)} %gather_fusion) | data formatting | bytes 16777216 | tf_op jit(solution)/shard_map/jit(_take)/gather | solution.py:79
  124.4 0.1 copy.48
  124.4 0.1 compare_and_fusion
  124.5 0.2 copy.49
  124.7 0.1 copy.45
  124.8 0.3 copy.46
  125.1 7.3 fusion
  132.4 189.9 %all_to_all.10 = bf16[8,32,4,4096]{3,2,0,1:T(4,128)(2,1)S(1)} all-to-all(bf16[8,32,4,4096]{3,2,0,1:T(4,128)(2,1)S(1)} %fusion), channel_id=1, replica_groups=mesh['expert'=32,'replica'=8] {'expert'}, dimensions={1} | all-to-all | bytes 16777216 | tf_op jit(solution)/shard_map/all_to_all | solution.py:82
  322.3 6.1 copy.51
  328.4 12.5 %reshape.149 = bf16[1024,4096]{1,0:T(8,128)(2,1)} reshape(bf16[8,32,4,4096]{3,2,1,0:T(4,128)(2,1)} %copy.51) | data formatting | bytes 16777216 | tf_op jit(solution)/shard_map/reshape | solution.py:44
  340.9 0.0 copy-start
  340.9 6.8 fusion.4
  347.8 0.0 copy-done
  347.8 0.0 copy-start.1
  347.8 5.1 abs_reduce_fusion
  352.9 0.0 copy-done.1
  352.9 5.6 convolution_convert_fusion
  358.6 0.0 copy-start.3
  358.6 0.0 copy-start.2
  358.6 0.0 reduce-scatter.2.cloned.1.call-update
  358.6 0.1 collective-permute-start.2
  358.7 2.9 collective-permute-start.1
  361.6 0.1 collective-permute-start
  361.7 0.0 copy-done.3
  361.7 0.1 add_reduce_fusion
  361.8 0.6 dynamic_slice.14
  363.1 0.2 fusion.16
  363.2 0.1 squeeze.24
  363.3 0.2 dynamic-slice_reduce_fusion
  363.5 0.1 squeeze.23
  363.6 0.0 copy-done.2
  363.7 233.9 %collective-permute-done.2 = bf16[1,192,4096]{2,1,0:T(8,128)(2,1)S(1)} collective-permute-done((bf16[1,192,4096]{2,1,0:T(8,128)(2,1)S(1)}, bf16[1,192,4096]{2,1,0:T(8,128)(2,1)S(1)}, u32[]{:S(2)}, u32[]{:S(2)}) %collective-permute-start.2) | collective-permute-done | bytes 1572896 | tf_op jit(solution)/shard_map/ppermute | solution.py:65
  597.6 1.3 broadcast_select_fusion
  598.9 0.0 reduce-scatter.2.cloned.1.call-done
  598.9 2.3 reshape.150
  601.1 99.3 %all-to-all-start.1 = ((bf16[32,4,4096]{2,1,0:T(4,128)(2,1)}), bf16[32,4,4096]{2,1,0:T(4,128)(2,1)S(1)}, u32[]{:S(2)}, u32[]{:S(2)}) async-start(bf16[32,4,4096]{2,1,0:T(4,128)(2,1)} %reshape.150), calls=%async_computation.2 | async-start | bytes 2097152 | tf_op jit(solution)/shard_map/all_to_all | solution.py:104
  700.5 0.0 collective-permute-done.1
  700.5 2.7 broadcast_select_fusion.1
  703.2 0.0 collective-permute-done
  703.2 2.7 broadcast_select_fusion.2
  705.9 34.1 %pmax.7 = f32[]{:T(128)} all-reduce(bf16[]{:T(256)} %get-tuple-element.13), channel_id=1, replica_groups=mesh['expert'=32,'replica'=8] {'replica'}, use_global_device_ids=true, to_apply=%region_10.11 | all-reduce | flops 1 | bytes 6 | tf_op jit(solution)/shard_map/pmax | solution.py:112
  740.0 0.0 collective-permute-start.3
  740.0 4.6 collective-permute-done.3
  745.9 0.0 all-to-all-done.1
  745.9 0.3 reshape.151
  746.2 0.9 gather_fusion.1
  747.1 1.1 multiply_reduce_fusion
  (9 shorter events, 0.1 us)
Async XLA Ops:
  7.2 591.7 %reduce-scatter.2.cloned.1.call-start = ((), (), s32[]{:S(2)}) async-start(), calls=%async_computation.3 | async-start | bytes 9437184 | tf_op jit(solution)/shard_map/reduce_scatter | solution.py:97
  340.9 6.9 copy-start
  347.8 5.1 copy-start.1
  358.6 3.1 copy-start.3
  358.6 5.1 copy-start.2
  358.6 239.0 %collective-permute-start.2 = (bf16[1,192,4096]{2,1,0:T(8,128)(2,1)S(1)}, bf16[1,192,4096]{2,1,0:T(8,128)(2,1)S(1)}, u32[]{:S(2)}, u32[]{:S(2)}) collective-permute-start(bf16[1,192,4096]{2,1,0:T(8,128)(2,1)S(1)} %copy-done.1), channel_id=1, source_target_pairs={{0,128},{8,136},{16,144},{24,152},{32,160},{40,168},{48,176},{56,1... | collective-permute-start | bytes 4718600 | tf_op jit(solution)/shard_map/ppermute | solution.py:65
  358.7 341.8 %collective-permute-start.1 = (bf16[1,192,4096]{2,1,0:T(8,128)(2,1)}, bf16[1,192,4096]{2,1,0:T(8,128)(2,1)}, u32[]{:S(2)}, u32[]{:S(2)}) collective-permute-start(bf16[1,192,4096]{2,1,0:T(8,128)(2,1)} %param.16), channel_id=1, source_target_pairs={{0,128},{8,136},{16,144},{24,152},{32,160},{40,168},{48,176},{56,1... | collective-permute-start | bytes 4718600 | tf_op jit(solution)/shard_map/ppermute | solution.py:65
  361.6 341.6 %collective-permute-start = (bf16[1,192,4096]{2,1,0:T(8,128)(2,1)}, bf16[1,192,4096]{2,1,0:T(8,128)(2,1)}, u32[]{:S(2)}, u32[]{:S(2)}) collective-permute-start(bf16[1,192,4096]{2,1,0:T(8,128)(2,1)} %param.15), channel_id=1, source_target_pairs={{0,128},{8,136},{16,144},{24,152},{32,160},{40,168},{48,176},{56,1... | collective-permute-start | bytes 4718600 | tf_op jit(solution)/shard_map/ppermute | solution.py:65
  601.1 144.8 %all-to-all-start.1 = ((bf16[32,4,4096]{2,1,0:T(4,128)(2,1)}), bf16[32,4,4096]{2,1,0:T(4,128)(2,1)S(1)}, u32[]{:S(2)}, u32[]{:S(2)}) async-start(bf16[32,4,4096]{2,1,0:T(4,128)(2,1)} %reshape.150), calls=%async_computation.2 | async-start | bytes 2097152 | tf_op jit(solution)/shard_map/all_to_all | solution.py:104
  740.0 4.6 collective-permute-start.3
Sparse Core Ops, SparseCore 0:
  358.7 222.3 reduce-scatter.1
where the time goes:
time: 757 us; the launch traced here: 756 us
  blocking collectives  315 us (42%)
  waiting for transfers between devices  238 us (31%)
  starting transfers between devices  102 us (13%)
  local copies, waits for them, and re-layouts  44.8 us (6%)
  other arithmetic  20.3 us (3%)
  matrix products  17.6 us (2%)
  between operations  17.3 us (2%)
    ppermute x3, waiting for transfers between devices, shards(): lax.ppermute(w, 'expert', ring)  234 us
    all_to_all x1, blocking collectives, shards(): lax.all_to_all(outgoing.reshape(replicas, experts, CAP, width), 'expert',...  190 us
    all_to_all x1, starting transfers between devices, shards(): lax.all_to_all(results, 'expert', split_axis=0, concat_axis=0, tiled=True)  99.3 us
    all_gather x1, blocking collectives, shards(): lax.all_gather(expert_ids, 'replica', axis=0, tiled=True)  46.4 us
    all_gather x1, blocking collectives, shards(): lax.all_gather(tokens, 'replica', axis=0, tiled=True)  44.8 us
    pmax x1, blocking collectives, shards(): group_peak = lax.pmax(local_peak, 'replica')  34.1 us
    gather x2, local copies, waits for them, and re-layouts, shards(): picked = jnp.take(group_tokens, source_all + starts, axis=0)  20.8 us
  transfers between devices with their start and end apart: 6, of which 2 were waited for; matrix products, arithmetic and copies ran while one was open for 1% of the time, Pallas kernels for 0%

commit v1 on v0

--- a/solution.py
+++ b/solution.py
@@ -69,7 +69,10 @@
     gate_local, up_local, down_local = (w_gate[0], w_up[0], w_down[0])
     group_tokens, group_ids = (
         lax.all_gather(tokens, "replica", axis=0, tiled=True),
-        lax.all_gather(expert_ids, "replica", axis=0, tiled=True),
+        jnp.concatenate(
+            lax.all_to_all(jnp.stack([expert_ids] * lax.axis_size("replica")), "replica", 0, 0),
+            axis=0,
+        ),
     )
     group_ids = group_ids.reshape(replicas, tok_rows, TOPK)
     slot_all, kept_all, source_all, filled_all = jax.vmap(route_slots, in_axes=(0, None, None))(

time: 757 us -> 723 us (0.955)
  blocking collectives: 315 us -> 269 us
  starting transfers between devices: 102 us -> 113 us
    all_gather x1 -> x0, blocking collectives: 46.4 us -> none  [shards(): lax.all_gather(expert_ids, 'replica', axis=0, tiled=True)]
    all_to_all x0 -> x1, starting transfers between devices: none -> 11.1 us  [shards(): lax.all_to_all(jnp.stack([expert_ids] * lax.axis_size('replica')), 'repli...]
  transfers between devices with their start and end apart: 6 -> 7, of which waited for: 2 -> 2; matrix products, arithmetic and copies ran while one was open for 1% -> 1% of each run, Pallas kernels for 0% -> 0%
where the time goes in v1:
time: 723 us; the launch traced here: 722 us
  blocking collectives  269 us (37%)
  waiting for transfers between devices  238 us (33%)
  starting transfers between devices  113 us (16%)
  local copies, waits for them, and re-layouts  46 us (6%)
  other arithmetic  20.3 us (3%)
  matrix products  17.6 us (2%)
  between operations  17.3 us (2%)
    ppermute x3, waiting for transfers between devices, shards(): lax.ppermute(w, 'expert', ring)  234 us
    all_to_all x1, blocking collectives, shards(): lax.all_to_all(outgoing.reshape(replicas, experts, CAP, width), 'expert',...  189 us
    all_to_all x1, starting transfers between devices, shards(): lax.all_to_all(results, 'expert', split_axis=0, concat_axis=0, tiled=True)  99.2 us
    all_gather x1, blocking collectives, shards(): lax.all_gather(tokens, 'replica', axis=0, tiled=True)  45.8 us
    pmax x1, blocking collectives, shards(): group_peak = lax.pmax(local_peak, 'replica')  34.1 us
    gather x2, local copies, waits for them, and re-layouts, shards(): picked = jnp.take(group_tokens, source_all + starts, axis=0)  20.8 us
  transfers between devices with their start and end apart: 7, of which 2 were waited for; matrix products, arithmetic and copies ran while one was open for 1% of the time, Pallas kernels for 0%

profile of v1, /device:TPU:4, one launch (start us, length us, event | category | flops | bytes accessed | tf_op | source)
XLA Modules:
  0.0 722.4 jit_solution(6869533828864325848)
XLA Ops:
  7.2 1.3 stack.2
  8.5 11.1 %all-to-all-start = ((s32[8,8,8]{2,1,0:T(8,128)}), s32[8,8,8]{2,1,0:T(8,128)S(1)}, u32[]{:S(2)}, u32[]{:S(2)}) async-start(s32[8,8,8]{2,1,0:T(8,128)} %stack.2), calls=%async_computation | async-start | bytes 65536 | tf_op jit(solution)/shard_map/all_to_all | solution.py:73
  19.6 0.0 reduce-scatter.2.cloned.1.call-start
  19.6 45.8 %all_gather.3 = bf16[64,4096]{1,0:T(8,128)(2,1)S(1)} all-gather(bf16[8,4096]{1,0:T(8,128)(2,1)} %param.9), channel_id=1, replica_groups=mesh['expert'=32,'replica'=8] {'replica'}, dimensions={0}, use_global_device_ids=true | all-gather | bytes 589824 | tf_op jit(solution)/shard_map/all_gather | solution.py:71
  65.5 0.0 all-to-all-done
  65.5 0.1 copy.49
  65.5 1.4 fusion.20
  66.9 3.0 select_reduce_fusion.1
  69.9 0.1 copy.41
  70.0 0.2 fusion.13
  70.2 0.2 select_reduce_fusion
  70.3 0.1 copy.44
  70.4 0.1 fusion.18
  70.5 7.7 %gather_fusion = bf16[1024,4096]{1,0:T(8,128)(2,1)} fusion(bf16[64,4096]{1,0:T(8,128)(2,1)S(1)} %all_gather.3, s32[1024]{0:T(1024)S(1)} %fusion.18), kind=kCustom, calls=%fused_computation | custom fusion | bytes 16781312 | tf_op jit(solution)/shard_map/jit(_take)/gather | solution.py:82
  78.2 13.1 %gather.13 = bf16[8,32,4,4096]{3,2,1,0:T(4,128)(2,1)} reshape(bf16[1024,4096]{1,0:T(8,128)(2,1)} %gather_fusion) | data formatting | bytes 16777216 | tf_op jit(solution)/shard_map/jit(_take)/gather | solution.py:82
  91.3 0.1 copy.45
  91.4 0.1 compare_and_fusion
  91.5 0.2 copy.46
  91.6 0.1 copy.42
  91.8 0.3 copy.43
  92.1 7.3 %fusion = bf16[8,32,4,4096]{3,2,0,1:T(4,128)(2,1)S(1)} fusion(bf16[8,32,4,4096]{3,2,1,0:T(4,128)(2,1)} %gather.13, pred[8,32,4]{2,0,1:T(8,128)(4,1)S(1)} %copy.46, pred[8,32,4]{2,0,1:T(8,128)(4,1)S(1)} %copy.43), kind=kLoop, calls=%fused_computation.3 | loop fusion | flops 8388608 | bytes 16779264 | tf_op jit(solution)/shard_map/jit(_where)/select_n | solution.py:83
  99.4 189.3 %all_to_all.15 = bf16[8,32,4,4096]{3,2,0,1:T(4,128)(2,1)S(1)} all-to-all(bf16[8,32,4,4096]{3,2,0,1:T(4,128)(2,1)S(1)} %fusion), channel_id=1, replica_groups=mesh['expert'=32,'replica'=8] {'expert'}, dimensions={1} | all-to-all | bytes 16777216 | tf_op jit(solution)/shard_map/all_to_all | solution.py:85
  288.7 6.1 copy.48
  294.8 12.5 %reshape.151 = bf16[1024,4096]{1,0:T(8,128)(2,1)} reshape(bf16[8,32,4,4096]{3,2,1,0:T(4,128)(2,1)} %copy.48) | data formatting | bytes 16777216 | tf_op jit(solution)/shard_map/reshape | solution.py:44
  307.4 0.0 copy-start
  307.4 6.8 fusion.4
  314.2 0.0 copy-done
  314.2 0.0 copy-start.1
  314.2 5.1 abs_reduce_fusion
  319.4 0.0 copy-done.1
  319.4 5.6 convolution_convert_fusion
  325.0 0.0 copy-start.3
  325.0 0.0 copy-start.2
  325.0 0.0 reduce-scatter.2.cloned.1.call-update
  325.0 0.1 collective-permute-start.2
  325.1 2.9 collective-permute-start.1
  328.0 0.1 collective-permute-start
  328.1 0.0 copy-done.3
  328.1 0.1 add_reduce_fusion
  328.2 0.6 dynamic_slice.14
  329.5 0.2 fusion.16
  329.7 0.1 squeeze.24
  329.7 0.2 dynamic-slice_reduce_fusion
  329.9 0.1 squeeze.23
  330.1 0.0 copy-done.2
  330.1 233.9 %collective-permute-done.2 = bf16[1,192,4096]{2,1,0:T(8,128)(2,1)S(1)} collective-permute-done((bf16[1,192,4096]{2,1,0:T(8,128)(2,1)S(1)}, bf16[1,192,4096]{2,1,0:T(8,128)(2,1)S(1)}, u32[]{:S(2)}, u32[]{:S(2)}) %collective-permute-start.2) | collective-permute-done | bytes 1572896 | tf_op jit(solution)/shard_map/ppermute | solution.py:65
  564.0 1.3 broadcast_select_fusion
  565.3 0.0 reduce-scatter.2.cloned.1.call-done
  565.3 2.3 reshape.152
  567.5 99.2 %all-to-all-start.2 = ((bf16[32,4,4096]{2,1,0:T(4,128)(2,1)}), bf16[32,4,4096]{2,1,0:T(4,128)(2,1)S(1)}, u32[]{:S(2)}, u32[]{:S(2)}) async-start(bf16[32,4,4096]{2,1,0:T(4,128)(2,1)} %reshape.152), calls=%async_computation.3 | async-start | bytes 2097152 | tf_op jit(solution)/shard_map/all_to_all | solution.py:107
  666.8 0.0 collective-permute-done.1
  666.8 2.7 broadcast_select_fusion.1
  669.5 0.0 collective-permute-done
  669.5 2.7 broadcast_select_fusion.2
  672.2 34.1 %pmax.7 = f32[]{:T(128)} all-reduce(bf16[]{:T(256)} %get-tuple-element.13), channel_id=1, replica_groups=mesh['expert'=32,'replica'=8] {'replica'}, use_global_device_ids=true, to_apply=%region_10.11 | all-reduce | flops 1 | bytes 6 | tf_op jit(solution)/shard_map/pmax | solution.py:115
  706.3 0.0 collective-permute-start.3
  706.3 4.6 collective-permute-done.3
  712.2 0.0 all-to-all-done.2
  712.2 0.3 reshape.153
  712.5 0.9 gather_fusion.1
  713.4 1.1 multiply_reduce_fusion
  (9 shorter events, 0.1 us)
Async XLA Ops:
  8.5 57.0 %all-to-all-start = ((s32[8,8,8]{2,1,0:T(8,128)}), s32[8,8,8]{2,1,0:T(8,128)S(1)}, u32[]{:S(2)}, u32[]{:S(2)}) async-start(s32[8,8,8]{2,1,0:T(8,128)} %stack.2), calls=%async_computation | async-start | bytes 65536 | tf_op jit(solution)/shard_map/all_to_all | solution.py:73
  19.6 545.7 %reduce-scatter.2.cloned.1.call-start = ((), (), s32[]{:S(2)}) async-start(), calls=%async_computation.4 | async-start | bytes 9437184 | tf_op jit(solution)/shard_map/reduce_scatter | solution.py:100
  307.4 6.9 copy-start
  314.2 5.1 copy-start.1
  325.0 3.1 copy-start.3
  325.0 5.1 copy-start.2
  325.0 239.0 %collective-permute-start.2 = (bf16[1,192,4096]{2,1,0:T(8,128)(2,1)S(1)}, bf16[1,192,4096]{2,1,0:T(8,128)(2,1)S(1)}, u32[]{:S(2)}, u32[]{:S(2)}) collective-permute-start(bf16[1,192,4096]{2,1,0:T(8,128)(2,1)S(1)} %copy-done.1), channel_id=1, source_target_pairs={{0,128},{8,136},{16,144},{24,152},{32,160},{40,168},{48,176},{56,1... | collective-permute-start | bytes 4718600 | tf_op jit(solution)/shard_map/ppermute | solution.py:65
  325.1 341.6 %collective-permute-start.1 = (bf16[1,192,4096]{2,1,0:T(8,128)(2,1)}, bf16[1,192,4096]{2,1,0:T(8,128)(2,1)}, u32[]{:S(2)}, u32[]{:S(2)}) collective-permute-start(bf16[1,192,4096]{2,1,0:T(8,128)(2,1)} %param.16), channel_id=1, source_target_pairs={{0,128},{8,136},{16,144},{24,152},{32,160},{40,168},{48,176},{56,1... | collective-permute-start | bytes 4718600 | tf_op jit(solution)/shard_map/ppermute | solution.py:65
  328.0 341.5 %collective-permute-start = (bf16[1,192,4096]{2,1,0:T(8,128)(2,1)}, bf16[1,192,4096]{2,1,0:T(8,128)(2,1)}, u32[]{:S(2)}, u32[]{:S(2)}) collective-permute-start(bf16[1,192,4096]{2,1,0:T(8,128)(2,1)} %param.15), channel_id=1, source_target_pairs={{0,128},{8,136},{16,144},{24,152},{32,160},{40,168},{48,176},{56,1... | collective-permute-start | bytes 4718600 | tf_op jit(solution)/shard_map/ppermute | solution.py:65
  567.5 144.6 %all-to-all-start.2 = ((bf16[32,4,4096]{2,1,0:T(4,128)(2,1)}), bf16[32,4,4096]{2,1,0:T(4,128)(2,1)S(1)}, u32[]{:S(2)}, u32[]{:S(2)}) async-start(bf16[32,4,4096]{2,1,0:T(4,128)(2,1)} %reshape.152), calls=%async_computation.3 | async-start | bytes 2097152 | tf_op jit(solution)/shard_map/all_to_all | solution.py:107
  706.3 4.6 collective-permute-start.3
Sparse Core Ops, SparseCore 0:
  325.1 222.2 reduce-scatter.1
